TPU v7x, 256 devices: a whole 4x4x8 slice. The times are simulated.
256 devices in a mesh: req: 32 (over y, z), tp: 8 (over x, core).
Axes of the slice: x: 4, y: 4, z: 8, core: 2. Of those that a mesh axis runs over, the one named last changes fastest.
Arguments:
- tokens: bfloat16 [32768, 1792], P(('req', 'tp')), may hold values from -6 to 6
- norm_gain: float32 [1792], replicated, may hold values from 0.25 to 1.75
- ffn_gain: float32 [1792], replicated, may hold values from 0.25 to 1.75
- mix_weight: bfloat16 [1792, 4, 1792], P('req', None, 'tp'), may hold values from -0.125 to 0.125
- out_weight: bfloat16 [1792, 1792], P('tp', 'req'), may hold values from -0.125 to 0.125
- ffn_weight: bfloat16 [1792, 2, 7168], P('req', None, 'tp'), may hold values from -0.125 to 0.125
- down_weight: bfloat16 [7168, 1792], P('tp', 'req'), may hold values from -0.0625 to 0.0625
- conv_taps: float32 [3, 1792], P(None, 'tp'), may hold values from -3 to 3
- past_cache: bfloat16 [32, 2, 64, 1792], P('req', None, None, 'tp'), may hold values from -210 to 210
- cached_len: int32 [32], P('req'), may hold values from 0 to 8192, as said below
Outputs:
- layer_out: bfloat16 [32768, 1792], P(('req', 'tp'))
- new_cache: bfloat16 [32, 2, 64, 1792], P('req', None, None, 'tp')
Inputs may be any that keep to these rules, and one draw needn't show every extreme that they name: `cached_len`: one request has exactly 8192 cached positions and another fewer than 64.
All inputs are finite; a program needn't handle non-finite values.
Results may differ from a plain program's by a relative error of at most 0.02.
Values may be sent and summed in bfloat16 or wider, within the bound.
No kernel may reach another device: no remote copies, remote signals or barrier semaphores. Data moves between devices by JAX's collectives and lax.ppermute only.
A program may use at most 64 MiB of HBM per device.

v0:
```python
import math
import jax
import jax.numpy as jnp
from jax import lax
from jax.sharding import PartitionSpec as P

HD = 112
WIN = 64


def normed(row_vals, gain):
    floats = row_vals.astype(jnp.float32)
    scaled = floats * lax.rsqrt(jnp.mean(floats * floats, axis=-1, keepdims=True) + 1e-05)
    return (scaled * gain).astype(jnp.bfloat16)


def window_attend(queries, key_rows, value_rows, length, window):
    row_count, head_count, head_size = queries.shape
    nb = row_count // window
    score_scale = 1.0 / math.sqrt(head_size)
    qb = queries.reshape(nb, window, head_count, head_size)

    def blocks(rows):
        lo = rows[:row_count].reshape(nb, window, head_count, head_size)
        hi = rows[window:].reshape(nb, window, head_count, head_size)
        return jnp.concatenate([lo, hi], axis=1)

    kb = blocks(key_rows)
    vb = blocks(value_rows)
    scores = jnp.einsum("bqhd,bkhd->bhqk", qb, kb, preferred_element_type=jnp.float32) * score_scale
    i = jnp.arange(window, dtype=jnp.int32)[:, None]
    j = jnp.arange(2 * window, dtype=jnp.int32)[None, :]
    b = jnp.arange(nb, dtype=jnp.int32)[:, None, None]
    usable = (j > i)[None] & (j <= i + window)[None] & (b * window + j >= window - length)
    scores = jnp.where(usable[:, None], scores, -1e30)
    row_max = jnp.max(scores, axis=-1, keepdims=True)
    exponent = jnp.exp(scores - row_max)
    weights = (exponent / jnp.sum(exponent, axis=-1, keepdims=True)).astype(jnp.bfloat16)
    out = jnp.einsum("bhqk,bkhd->bqhd", weights, vb, preferred_element_type=jnp.float32)
    return out.reshape(row_count, head_count, head_size)


def mix_request(projected, cache_rows, length, tap_table, window, head_size):
    row_count, feat_width = (projected.shape[0], projected.shape[2])
    time_order = (length + jnp.arange(window, dtype=jnp.int32)) % window
    earlier = cache_rows[:, time_order]
    key_rows = jnp.concatenate([earlier[0], projected[:, 1]], axis=0)
    value_rows = jnp.concatenate([earlier[1], projected[:, 2]], axis=0)
    head_count = feat_width // head_size
    attended = window_attend(
        projected[:, 0].reshape(row_count, head_count, head_size),
        key_rows.reshape(-1, head_count, head_size),
        value_rows.reshape(-1, head_count, head_size),
        length,
        window,
    ).reshape(row_count, feat_width)
    positions = jnp.arange(window + row_count, dtype=jnp.int32)
    alive_mask = (positions >= window - length)[:, None]
    masked_values = jnp.where(alive_mask, value_rows.astype(jnp.float32), jnp.float32(0.0))
    tap_count = tap_table.shape[0]
    convolved = jnp.zeros((row_count, feat_width), jnp.float32)
    for tap_index in range(tap_count):
        begin_row = window - (tap_count - 1) + tap_index
        convolved = (
            convolved + tap_table[tap_index] * masked_values[begin_row : begin_row + row_count]
        )
    mixed_heads = (attended + projected[:, 3].astype(jnp.float32) * convolved).astype(jnp.bfloat16)
    slot_source = (
        row_count - window + (jnp.arange(window, dtype=jnp.int32) - length - row_count) % window
    )
    renewed = jnp.stack([projected[:, 1], projected[:, 2]])[:, slot_source]
    return (mixed_heads, renewed)


def gather_weights(mix_weight, out_weight, ffn_weight, down_weight):
    rows = mix_weight.shape[0]
    pieces = [
        mix_weight.reshape(rows, -1),
        ffn_weight.reshape(rows, -1),
        down_weight.T,
        out_weight.T,
    ]
    widths = [p.shape[1] for p in pieces]
    got = lax.all_gather(jnp.concatenate(pieces, axis=1), "req", axis=0, tiled=True)
    parts = []
    start = 0
    for w in widths:
        parts.append(got[:, start : start + w])
        start += w
    return parts


def tp_gather(x):
    n = lax.axis_size("tp")
    return lax.all_to_all(jnp.tile(x, (n, 1)), "tp", 0, 0, tiled=True)


def tp_sum_scatter(x):
    n = lax.axis_size("tp")
    got = lax.all_to_all(x, "tp", 0, 0, tiled=True)
    return got.reshape((n, -1) + x.shape[1:]).astype(jnp.float32).sum(axis=0)


def local(
    tokens,
    norm_gain,
    ffn_gain,
    mix_weight,
    out_weight,
    ffn_weight,
    down_weight,
    conv_taps,
    past_cache,
    cached_len,
):
    feat_width = mix_weight.shape[2]
    ffn_width = ffn_weight.shape[2]
    mix_all, ffn_all, down_t, out_t = gather_weights(
        mix_weight, out_weight, ffn_weight, down_weight
    )
    normed_all = tp_gather(normed(tokens, norm_gain))
    row_total = normed_all.shape[0]
    projected = jnp.dot(normed_all, mix_all, preferred_element_type=jnp.float32)
    projected = projected.astype(jnp.bfloat16).reshape(row_total, 4, feat_width)
    mixed_heads, renewed = mix_request(projected, past_cache[0], cached_len[0], conv_taps, WIN, HD)
    attn_full = lax.dot_general(
        mixed_heads, out_t, (((1,), (1,)), ((), ())), preferred_element_type=jnp.float32
    )
    attn_part = tp_sum_scatter(attn_full.astype(jnp.bfloat16))
    residual = (tokens.astype(jnp.float32) + attn_part).astype(jnp.bfloat16)
    ffn_in = tp_gather(normed(residual, ffn_gain))
    gate_up = jnp.dot(ffn_in, ffn_all, preferred_element_type=jnp.float32)
    activated = (jax.nn.silu(gate_up[:, :ffn_width]) * gate_up[:, ffn_width:]).astype(jnp.bfloat16)
    ffn_full = lax.dot_general(
        activated, down_t, (((1,), (1,)), ((), ())), preferred_element_type=jnp.float32
    )
    ffn_part = tp_sum_scatter(ffn_full.astype(jnp.bfloat16))
    layer_out = (residual.astype(jnp.float32) + ffn_part).astype(jnp.bfloat16)
    return (layer_out, renewed[None])


def solution(mesh):
    in_specs = (
        P(("req", "tp"), None),
        P(),
        P(),
        P("req", None, "tp"),
        P("tp", "req"),
        P("req", None, "tp"),
        P("tp", "req"),
        P(None, "tp"),
        P("req", None, None, "tp"),
        P("req"),
    )
    out_specs = (P(("req", "tp"), None), P("req", None, None, "tp"))
    return jax.shard_map(local, mesh=mesh, in_specs=in_specs, out_specs=out_specs, check_vma=False)
```

profile of v0, /device:TPU:1, one launch (start us, length us, event | category | flops | bytes accessed | tf_op | source)
XLA Modules:
  0.0 342.7 jit_solution(4850070380336900980)
XLA Ops:
  9.2 1.7 pad_maximum_fusion.3
  12.2 1.2 fusion.22
  13.4 2.0 tile.4
  15.4 7.8 %all-to-all-start = ((bf16[8,128,1792]{2,1,0:T(8,128)(2,1)}), bf16[8,128,1792]{2,1,0:T(8,128)(2,1)}, u32[]{:S(2)}, u32[]{:S(2)}) async-start(bf16[8,128,1792]{2,1,0:T(8,128)(2,1)} %tile.4), calls=%async_computation | async-start | bytes 7340032 | tf_op jit(solution)/shard_map/all_to_all | solution.py:95
  25.2 41.3 %all-to-all-done = bf16[8,128,1792]{2,1,0:T(8,128)(2,1)} async-done(((bf16[8,128,1792]{2,1,0:T(8,128)(2,1)}), bf16[8,128,1792]{2,1,0:T(8,128)(2,1)}, u32[]{:S(2)}, u32[]{:S(2)}) %all-to-all-start) | async-done | bytes 3670048 | tf_op jit(solution)/shard_map/all_to_all | solution.py:95
  66.5 73.7 %all-gather.2.cloned.1.call-done = bf16[1792,3808]{1,0:T(8,128)(2,1)} async-done(((bf16[56,3808]{1,0:T(8,128)(2,1)}), bf16[1792,3808]{1,0:T(8,128)(2,1)}) %all-gather.2.cloned.1.call-update) | async-done | bytes 13647888 | tf_op jit(solution)/shard_map/all_gather | solution.py:84
  140.2 6.6 %fusion.9 = bf16[1024,896]{0,1:T(8,128)(2,1)S(1)} fusion(bf16[1024,1792]{1,0:T(8,128)(2,1)} %bitcast.4, bf16[1792,3808]{1,0:T(8,128)(2,1)} %all-gather.2.cloned.1.call-done), kind=kOutput, calls=%fused_computation.15 | convolution fusion | flops 3289251840 | bytes 8716288 | tf_op jit(solution)/shard_map/dot_general | solution.py:123
  146.7 1.2 slice_bitcast_fusion
  149.0 1.5 reshape.281
  150.5 1.7 reshape.283
  152.5 2.5 fusion.63
  155.0 3.0 fusion.14
  158.9 1.2 copy.28
  160.1 1.2 copy.29
  162.4 6.3 %convolution_bitcast_fusion = f32[16,64,2,112]{3,1,2,0:T(8,128)S(1)} fusion(bf16[16,64,2,112]{1,3,2,0:T(8,128)(2,1)} %copy.29, bf16[16,64,2,112]{1,3,2,0:T(8,128)(2,1)} %copy.28, f32[16,2,64]{2,1,0:T(2,128)S(1)} %fusion.63, f32[16,2,64,128]{3,2,1,0:T(8,128)} %fusion.14), kind=kOutput, calls=%fused_computation.26 | convolution fusion | flops 61343872 | bytes 2891776 | tf_op jit(solution)/shard_map/bhqk,bkhd->bqhd/dot_general | solution.py:39
  170.3 2.9 convolution_convert_fusion.1
  173.2 48.7 %all_to_all.36 = bf16[8,128,1792]{2,1,0:T(8,128)(2,1)S(1)} all-to-all(bf16[8,128,1792]{2,1,0:T(8,128)(2,1)S(1)} %bitcast.59), channel_id=1, replica_groups=mesh['req'=32,'tp'=8] {'tp'}, dimensions={0} | all-to-all | bytes 7340032 | tf_op jit(solution)/shard_map/all_to_all | solution.py:100
  223.6 47.2 %all_to_all.37 = bf16[8,128,1792]{2,1,0:T(8,128)(2,1)S(1)} all-to-all(bf16[8,128,1792]{2,1,0:T(8,128)(2,1)S(1)} %tile.5), channel_id=1, replica_groups=mesh['req'=32,'tp'=8] {'tp'}, dimensions={0} | all-to-all | bytes 7340032 | tf_op jit(solution)/shard_map/all_to_all | solution.py:95
  270.8 6.8 %fusion.1 = f32[1024,1792]{1,0:T(8,128)S(1)} fusion(bf16[1024,1792]{1,0:T(8,128)(2,1)S(1)} %bitcast.60, bf16[1792,3808]{1,0:T(8,128)(2,1)S(1)} %bitcast.76), kind=kOutput, calls=%fused_computation.5 | convolution fusion | flops 6576668672 | bytes 17432576 | tf_op jit(solution)/shard_map/dot_general | solution.py:132
  277.7 6.0 %convolution_convert_fusion = bf16[1024,1792]{1,0:T(8,128)(2,1)} fusion(bf16[1792,3808]{1,0:T(8,128)(2,1)S(1)} %bitcast.76, f32[1024,1792]{1,0:T(8,128)S(1)} %fusion.1), kind=kOutput, calls=%fused_computation.7 | convolution fusion | flops 3295674368 | bytes 14221312 | tf_op jit(solution)/shard_map/dot_general | solution.py:134
  283.6 5.4 %all-to-all-start.3 = ((bf16[8,128,1792]{2,1,0:T(8,128)(2,1)}), bf16[8,128,1792]{2,1,0:T(8,128)(2,1)}, u32[]{:S(2)}, u32[]{:S(2)}) async-start(bf16[8,128,1792]{2,1,0:T(8,128)(2,1)} %bitcast.58), calls=%async_computation.3 | async-start | bytes 7340032 | tf_op jit(solution)/shard_map/all_to_all | solution.py:100
  290.7 2.6 pad_maximum_fusion
  294.7 37.6 %all-to-all-done.3 = bf16[8,128,1792]{2,1,0:T(8,128)(2,1)} async-done(((bf16[8,128,1792]{2,1,0:T(8,128)(2,1)}), bf16[8,128,1792]{2,1,0:T(8,128)(2,1)}, u32[]{:S(2)}, u32[]{:S(2)}) %all-to-all-start.3) | async-done | bytes 3670048 | tf_op jit(solution)/shard_map/all_to_all | solution.py:100
  332.4 2.6 convert_reduce_fusion
  (64 shorter events, 14.8 us)
Async XLA Ops:
  7.2 133.0 %all-gather.2.cloned.1.call-start = ((), (), s32[]{:S(2)}) async-start(), calls=%async_computation.4 | async-start | bytes 14192640 | tf_op jit(solution)/shard_map/all_gather | solution.py:84
  15.4 8.4 %copy-start.3 = (bf16[1,2,64,224]{3,2,1,0:T(8,128)(2,1)S(1)}, bf16[1,2,64,224]{3,2,1,0:T(8,128)(2,1)}, u32[]{:S(2)}) copy-start(bf16[1,2,64,224]{3,2,1,0:T(8,128)(2,1)} %param.18) | copy-start | bytes 172036
  15.4 9.6 %copy-start.5 = (f32[3,224]{1,0:T(4,128)S(1)}, f32[3,224]{1,0:T(4,128)}, u32[]{:S(2)}) copy-start(f32[3,224]{1,0:T(4,128)} %param.17) | copy-start | bytes 8068
  15.4 51.1 %all-to-all-start = ((bf16[8,128,1792]{2,1,0:T(8,128)(2,1)}), bf16[8,128,1792]{2,1,0:T(8,128)(2,1)}, u32[]{:S(2)}, u32[]{:S(2)}) async-start(bf16[8,128,1792]{2,1,0:T(8,128)(2,1)} %tile.4), calls=%async_computation | async-start | bytes 7340032 | tf_op jit(solution)/shard_map/all_to_all | solution.py:95
  152.4 5.5 %copy-start.2 = (bf16[1024,1,224]{0,2,1:T(8,128)(2,1)S(1)}, bf16[1024,1,224]{0,2,1:T(8,128)(2,1)}, u32[]{:S(2)}) copy-start(bf16[1024,1,224]{0,2,1:T(8,128)(2,1)} %get-tuple-element.10) | copy-start | bytes 1376260
  158.0 3.4 copy-start.1
  170.3 100.5 %slice-start = ((s8[13762560]{0:T(1024)(128)(4,1)}), s8[4194304]{0:T(1024)(128)(4,1)S(1)}, s32[]{:S(2)}) async-start(s8[13762560]{0:T(1024)(128)(4,1)} %bitcast.75), calls=%async_computation.5 | async-start | bytes 8388608
  170.3 100.5 %slice-start.1 = ((s8[13762560]{0:T(1024)(128)(4,1)}), s8[4194304]{0:T(1024)(128)(4,1)S(1)}, s32[]{:S(2)}) async-start(s8[13762560]{0:T(1024)(128)(4,1)} %bitcast.75), calls=%async_computation.6 | async-start | bytes 8388608
  221.9 1.0 copy-start
  221.9 1.2 copy-start.4
  221.9 48.9 %slice-start.2 = ((s8[13762560]{0:T(1024)(128)(4,1)}), s8[4194304]{0:T(1024)(128)(4,1)S(1)}, s32[]{:S(2)}) async-start(s8[13762560]{0:T(1024)(128)(4,1)} %bitcast.75), calls=%async_computation.7 | async-start | bytes 8388608
  223.3 47.5 %slice-start.3 = ((s8[13762560]{0:T(1024)(128)(4,1)}), s8[1179648]{0:T(1024)(128)(4,1)S(1)}, s32[]{:S(2)}) async-start(s8[13762560]{0:T(1024)(128)(4,1)} %bitcast.75), calls=%async_computation.8 | async-start | bytes 2359296
  283.6 48.7 %all-to-all-start.3 = ((bf16[8,128,1792]{2,1,0:T(8,128)(2,1)}), bf16[8,128,1792]{2,1,0:T(8,128)(2,1)}, u32[]{:S(2)}, u32[]{:S(2)}) async-start(bf16[8,128,1792]{2,1,0:T(8,128)(2,1)} %bitcast.58), calls=%async_computation.3 | async-start | bytes 7340032 | tf_op jit(solution)/shard_map/all_to_all | solution.py:100
Sparse Core Ops, SparseCore 0:
  11.2 128.9 all-gather.1
where the time goes:
time: 343 us
  waiting for transfers between devices  153 us (45%)
  blocking collectives  95.9 us (28%)
  matrix products  34 us (10%)
  local copies, waits for them, and re-layouts  20 us (6%)
  between operations  15 us (4%)
  starting transfers between devices  13.2 us (4%)
  other arithmetic  11.9 us (3%)
    all_gather x1, waiting for transfers between devices, gather_weights(): lax.all_gather(jnp.concatenate(pieces, axis=1), 'req', axis=0, tiled=True)  73.7 us
    all_to_all x1, blocking collectives, tp_sum_scatter(): got = lax.all_to_all(x, 'tp', 0, 0, tiled=True)  48.7 us
    all_to_all x1, blocking collectives, tp_gather(): return lax.all_to_all(jnp.tile(x, (n, 1)), 'tp', 0, 0, tiled=True)  47.2 us
    all_to_all x1, waiting for transfers between devices, tp_gather(): return lax.all_to_all(jnp.tile(x, (n, 1)), 'tp', 0, 0, tiled=True)  41.3 us
    all_to_all x1, waiting for transfers between devices, tp_sum_scatter(): got = lax.all_to_all(x, 'tp', 0, 0, tiled=True)  37.6 us
    all_to_all x1, starting transfers between devices, tp_gather(): return lax.all_to_all(jnp.tile(x, (n, 1)), 'tp', 0, 0, tiled=True)  7.76 us
  transfers between devices with their start and end apart: 3, of which 3 were waited for; matrix products, arithmetic and copies ran while one was open for 3% of the time, Pallas kernels for 0%

commit v1 on v0

--- a/solution.py
+++ b/solution.py
@@ -81,7 +81,9 @@
         out_weight.T,
     ]
     widths = [p.shape[1] for p in pieces]
-    got = lax.all_gather(jnp.concatenate(pieces, axis=1), "req", axis=0, tiled=True)
+    block = jnp.concatenate(pieces, axis=1)
+    repeated = jnp.stack([block] * lax.axis_size("req"))
+    got = jnp.concatenate(lax.all_to_all(repeated, "req", 0, 0), axis=0)
     parts = []
     start = 0
     for w in widths:

time: 343 us -> 599 us (1.75)
  the two profiles are of different devices: /device:TPU:1 before, /device:TPU:184 now
where the time goes in v1:
time: 599 us; the launch traced here: 598 us
  waiting for transfers between devices  407 us (68%)
  blocking collectives  95 us (16%)
  matrix products  36.6 us (6%)
  local copies, waits for them, and re-layouts  26.3 us (4%)
  starting transfers between devices  18.7 us (3%)
  other arithmetic  12.3 us (2%)
    all_to_all x1, waiting for transfers between devices, gather_weights(): got = jnp.concatenate(lax.all_to_all(repeated, 'req', 0, 0), axis=0)  327 us
    all_to_all x1, blocking collectives, tp_sum_scatter(): got = lax.all_to_all(x, 'tp', 0, 0, tiled=True)  47.9 us
    all_to_all x1, blocking collectives, tp_gather(): return lax.all_to_all(jnp.tile(x, (n, 1)), 'tp', 0, 0, tiled=True)  47.1 us
    all_to_all x1, waiting for transfers between devices, tp_gather(): return lax.all_to_all(jnp.tile(x, (n, 1)), 'tp', 0, 0, tiled=True)  43.8 us
    all_to_all x1, waiting for transfers between devices, tp_sum_scatter(): got = lax.all_to_all(x, 'tp', 0, 0, tiled=True)  36.3 us
  transfers between devices with their start and end apart: 3, of which 3 were waited for; matrix products, arithmetic and copies ran while one was open for 2% of the time, Pallas kernels for 0%

profile of v1, /device:TPU:184, one launch (start us, length us, event | category | flops | bytes accessed | tf_op | source)
XLA Modules:
  0.0 598.0 jit_solution(1000163553284832044)
XLA Ops:
  3.0 2.0 tile.4
  5.1 4.6 all-to-all-start
  10.0 43.8 %all-to-all-done = bf16[8,128,1792]{2,1,0:T(8,128)(2,1)} async-done(((bf16[8,128,1792]{2,1,0:T(8,128)(2,1)}), bf16[8,128,1792]{2,1,0:T(8,128)(2,1)}, u32[]{:S(2)}, u32[]{:S(2)}) %all-to-all-start) | async-done | bytes 3670048 | tf_op jit(solution)/shard_map/all_to_all | solution.py:97
  53.8 5.9 stack.4
  59.6 9.5 %all-to-all-start.1 = ((bf16[32,56,3808]{2,1,0:T(8,128)(2,1)}), bf16[32,56,3808]{2,1,0:T(8,128)(2,1)}, u32[]{:S(2)}, u32[]{:S(2)}) async-start(bf16[32,56,3808]{2,1,0:T(8,128)(2,1)} %stack.4), calls=%async_computation.1 | async-start | bytes 27525120 | tf_op jit(solution)/shard_map/all_to_all | solution.py:86
  71.7 327.3 %all-to-all-done.1 = bf16[32,56,3808]{2,1,0:T(8,128)(2,1)} async-done(((bf16[32,56,3808]{2,1,0:T(8,128)(2,1)}), bf16[32,56,3808]{2,1,0:T(8,128)(2,1)}, u32[]{:S(2)}, u32[]{:S(2)}) %all-to-all-start.1) | async-done | bytes 13647904 | tf_op jit(solution)/shard_map/all_to_all | solution.py:86
  398.9 6.6 %fusion.9 = bf16[1024,896]{0,1:T(8,128)(2,1)S(1)} fusion(bf16[1024,1792]{1,0:T(8,128)(2,1)} %bitcast.4, bf16[1792,3808]{1,0:T(8,128)(2,1)} %bitcast.7), kind=kOutput, calls=%fused_computation.15 | convolution fusion | flops 3289251840 | bytes 8716288 | tf_op jit(solution)/shard_map/dot_general | solution.py:125
  405.5 1.3 slice_bitcast_fusion
  407.9 1.7 reshape.289
  409.8 1.7 reshape.287
  411.5 1.8 fusion.14
  413.3 1.9 fusion.63
  419.2 6.0 %convolution_bitcast_fusion = f32[16,64,2,112]{3,1,2,0:T(8,128)S(1)} fusion(bf16[16,64,2,112]{1,3,2,0:T(8,128)(2,1)S(1)} %copy.29, bf16[16,64,2,112]{1,3,2,0:T(8,128)(2,1)} %copy.28, f32[16,2,64]{2,1,0:T(2,128)} %fusion.63, f32[16,2,64,128]{3,2,1,0:T(8,128)} %fusion.14), kind=kOutput, calls=%fused_computation.26 | convolution fusion | flops 61343872 | bytes 2891776 | tf_op jit(solution)/shard_map/bhqk,bkhd->bqhd/dot_general | solution.py:39
  426.0 1.6 reshape_reshape.3
  428.8 2.9 convolution_convert_fusion.1
  431.7 47.9 %all_to_all.41 = bf16[8,128,1792]{2,1,0:T(8,128)(2,1)S(1)} all-to-all(bf16[8,128,1792]{2,1,0:T(8,128)(2,1)S(1)} %bitcast.60), channel_id=1, replica_groups=mesh['req'=32,'tp'=8] {'tp'}, dimensions={0} | all-to-all | bytes 7340032 | tf_op jit(solution)/shard_map/all_to_all | solution.py:102
  481.3 47.1 %all_to_all.42 = bf16[8,128,1792]{2,1,0:T(8,128)(2,1)S(1)} all-to-all(bf16[8,128,1792]{2,1,0:T(8,128)(2,1)S(1)} %tile.5), channel_id=1, replica_groups=mesh['req'=32,'tp'=8] {'tp'}, dimensions={0} | all-to-all | bytes 7340032 | tf_op jit(solution)/shard_map/all_to_all | solution.py:97
  528.4 9.6 %fusion.1 = f32[1024,1792]{1,0:T(8,128)S(1)} fusion(bf16[1024,1792]{1,0:T(8,128)(2,1)S(1)} %bitcast.61, bf16[1792,3808]{1,0:T(8,128)(2,1)} %bitcast.7), kind=kOutput, calls=%fused_computation.5 | convolution fusion | flops 6576668672 | bytes 17432576 | tf_op jit(solution)/shard_map/dot_general | solution.py:134
  538.1 7.8 %convolution_convert_fusion = bf16[1024,1792]{1,0:T(8,128)(2,1)} fusion(bf16[1792,3808]{1,0:T(8,128)(2,1)} %bitcast.7, f32[1024,1792]{1,0:T(8,128)S(1)} %fusion.1), kind=kOutput, calls=%fused_computation.7 | convolution fusion | flops 3295674368 | bytes 14221312 | tf_op jit(solution)/shard_map/dot_general | solution.py:136
  545.9 4.6 all-to-all-start.4
  552.2 3.4 pad_maximum_fusion
  555.6 1.9 gather_fusion.1
  558.2 36.3 %all-to-all-done.4 = bf16[8,128,1792]{2,1,0:T(8,128)(2,1)} async-done(((bf16[8,128,1792]{2,1,0:T(8,128)(2,1)}), bf16[8,128,1792]{2,1,0:T(8,128)(2,1)}, u32[]{:S(2)}, u32[]{:S(2)}) %all-to-all-start.4) | async-done | bytes 3670048 | tf_op jit(solution)/shard_map/all_to_all | solution.py:102
  594.6 2.6 convert_reduce_fusion
  (65 shorter events, 16.4 us)
Async XLA Ops:
  5.1 4.7 copy-start.3
  5.1 4.7 copy-start.4
  5.1 4.8 copy-start.5
  5.1 4.9 copy-start.7
  5.1 48.7 %all-to-all-start = ((bf16[8,128,1792]{2,1,0:T(8,128)(2,1)}), bf16[8,128,1792]{2,1,0:T(8,128)(2,1)}, u32[]{:S(2)}, u32[]{:S(2)}) async-start(bf16[8,128,1792]{2,1,0:T(8,128)(2,1)} %tile.4), calls=%async_computation | async-start | bytes 7340032 | tf_op jit(solution)/shard_map/all_to_all | solution.py:97
  59.6 10.1 %copy-start.6 = (bf16[1,2,64,224]{3,2,1,0:T(8,128)(2,1)S(1)}, bf16[1,2,64,224]{3,2,1,0:T(8,128)(2,1)}, u32[]{:S(2)}) copy-start(bf16[1,2,64,224]{3,2,1,0:T(8,128)(2,1)} %param.18) | copy-start | bytes 172036
  59.6 11.9 %copy-start.9 = (f32[3,224]{1,0:T(4,128)S(1)}, f32[3,224]{1,0:T(4,128)}, u32[]{:S(2)}) copy-start(f32[3,224]{1,0:T(4,128)} %param.17) | copy-start | bytes 8068
  59.6 339.3 %all-to-all-start.1 = ((bf16[32,56,3808]{2,1,0:T(8,128)(2,1)}), bf16[32,56,3808]{2,1,0:T(8,128)(2,1)}, u32[]{:S(2)}, u32[]{:S(2)}) async-start(bf16[32,56,3808]{2,1,0:T(8,128)(2,1)} %stack.4), calls=%async_computation.1 | async-start | bytes 27525120 | tf_op jit(solution)/shard_map/all_to_all | solution.py:86
  71.4 345.4 %copy-start.2 = (bf16[1,64,224]{2,1,0:T(8,128)(2,1)}, bf16[1,64,224]{2,1,0:T(8,128)(2,1)S(1)}, u32[]{:S(2)}) copy-start(bf16[1,64,224]{2,1,0:T(8,128)(2,1)S(1)} %copy.65) | copy-start | bytes 86020
  425.2 3.4 copy-start.1
  479.6 1.0 copy-start
  479.6 1.2 copy-start.8
  545.9 4.6 copy-start.10
  545.9 48.7 %all-to-all-start.4 = ((bf16[8,128,1792]{2,1,0:T(8,128)(2,1)}), bf16[8,128,1792]{2,1,0:T(8,128)(2,1)}, u32[]{:S(2)}, u32[]{:S(2)}) async-start(bf16[8,128,1792]{2,1,0:T(8,128)(2,1)} %bitcast.59), calls=%async_computation.4 | async-start | bytes 7340032 | tf_op jit(solution)/shard_map/all_to_all | solution.py:102
